TPU v7x, 512 devices: a whole 4x8x8 slice. The times are simulated.
512 devices in a mesh: dp: 16 (over y, core), tensor: 32 (over z, x).
Axes of the slice: x: 4, y: 8, z: 8, core: 2. Of those that a mesh axis runs over, the one named last changes fastest.
Arguments:
- layer_input: bfloat16 [65536, 8192], P('dp', 'tensor'), may hold values from -6 to 6
- output_grad: bfloat16 [65536, 1024], P(('dp', 'tensor')), may hold values from -6 to 6
- key_weight: bfloat16 [8192, 1024], P('tensor'), may hold values from -0.0625 to 0.0625
- adapter_down: bfloat16 [128, 16, 8192], P('dp', None, 'tensor'), may hold values from -0.0625 to 0.0625
- adapter_up: bfloat16 [128, 16, 1024], P('dp', None, 'tensor'), may hold values from -0.1875 to 0.1875
- segment_adapter: int32 [512], replicated, may hold values from 0 to 127
- adapter_slot: int32 [128], replicated, may hold values from 0 to 127, each once
- live_segments: int32 [16], P('dp'), may hold values from 1 to 32, as said below
Outputs:
- input_grad: bfloat16 [65536, 8192], P('dp', 'tensor')
- down_grad: bfloat16 [128, 16, 8192], P('dp', None, 'tensor')
- up_grad: bfloat16 [128, 16, 1024], P('dp', None, 'tensor')
Inputs may be any that keep to these rules, and one draw needn't show every extreme that they name: `live_segments`: some data group has all 32 segments live; a group's segments at or past its count are padding.
All inputs are finite; a program needn't handle non-finite values.
Results may differ from a plain program's by a relative error of at most 0.0057.
Values may be sent and summed in bfloat16 or wider, within the bound.
No kernel may reach another device: no remote copies, remote signals or barrier semaphores. Data moves between devices by JAX's collectives and lax.ppermute only.
A program may use at most 64 MiB of HBM per device.

v0:
```python
import jax
import jax.numpy as jnp
from jax import lax
from jax.sharding import PartitionSpec as P


def on_device(
    layer_input,
    output_grad,
    key_weight,
    adapter_down,
    adapter_up,
    segment_adapter,
    adapter_slot,
    live_segments,
):
    tensor_size = lax.axis_size("tensor")
    position = lax.axis_index("tensor")
    group_count = lax.axis_size("dp")
    group_index = lax.axis_index("dp")
    tok_group = layer_input.shape[0]
    width_shard = layer_input.shape[1]
    key_width = output_grad.shape[1]
    key_shard = key_width // tensor_size
    adapters = adapter_slot.shape[0]
    rank_dim = adapter_down.shape[1]
    seg_total = segment_adapter.shape[0]
    seg_group = seg_total // group_count
    seg_len = tok_group // seg_group
    whole_raw = lax.all_gather(output_grad, "tensor", axis=0, tiled=True)
    slot_ids = jnp.arange(adapters, dtype=jnp.int32)
    lookup = segment_adapter[:, None] == slot_ids[None, :]
    every_slot = jnp.sum(jnp.where(lookup, adapter_slot[None, :], 0), axis=1)
    seg_slot = lax.dynamic_slice_in_dim(every_slot, group_index * seg_group, seg_group)
    seg_live = jnp.arange(seg_group, dtype=jnp.int32) < live_segments[0]
    local_store = jnp.concatenate([adapter_down, adapter_up], axis=2)
    stores = lax.all_gather(local_store, "dp", axis=0, tiled=True)
    choose = (seg_slot[:, None] == slot_ids[None, :]).astype(jnp.bfloat16)
    seg_store = jnp.dot(choose, stores.reshape(adapters, -1), preferred_element_type=jnp.float32)
    seg_store = seg_store.astype(jnp.bfloat16).reshape(seg_group, rank_dim, width_shard + key_shard)
    down_seg = seg_store[:, :, :width_shard]
    up_seg = seg_store[:, :, width_shard:]
    whole = jnp.where(jnp.repeat(seg_live, seg_len)[:, None], whole_raw, jnp.zeros_like(whole_raw))
    own_keys = lax.dynamic_slice_in_dim(whole, position * key_shard, key_shard, 1).reshape(
        seg_group, seg_len, key_shard
    )
    input_seg = layer_input.reshape(seg_group, seg_len, width_shard)
    up_part = jnp.einsum("sjk,srk->srj", own_keys, up_seg, preferred_element_type=jnp.float32)
    down_part = jnp.einsum("sjd,srd->srj", input_seg, down_seg, preferred_element_type=jnp.float32)
    both = lax.psum(jnp.stack([up_part, down_part]), "tensor")
    both = lax.reduce_precision(both, exponent_bits=8, mantissa_bits=7)
    lowrank = both[0].astype(jnp.bfloat16)
    projected = both[1].astype(jnp.bfloat16)
    frozen = lax.dot_general(
        whole, key_weight, (((1,), (1,)), ((), ())), preferred_element_type=jnp.float32
    )
    extra = jnp.einsum("srj,srd->sjd", lowrank, down_seg, preferred_element_type=jnp.float32)
    input_grad = (frozen + 2.0 * extra.reshape(tok_group, width_shard)).astype(jnp.bfloat16)
    seg_down = 2.0 * jnp.einsum(
        "srj,sjd->srd", lowrank, input_seg, preferred_element_type=jnp.float32
    )
    seg_up = 2.0 * jnp.einsum(
        "srj,sjk->srk", projected, own_keys, preferred_element_type=jnp.float32
    )
    seg_grad = jnp.concatenate([seg_down, seg_up], axis=2)
    onehot = (seg_slot[:, None] == slot_ids[None, :]).astype(jnp.float32)
    part = jnp.einsum("sa,srd->ard", onehot, seg_grad, precision=lax.Precision.HIGHEST)
    part = lax.reduce_precision(part, exponent_bits=8, mantissa_bits=7)
    total = lax.psum_scatter(part, "dp", scatter_dimension=0, tiled=True)
    down_grad = total[:, :, :width_shard].astype(jnp.bfloat16)
    up_grad = total[:, :, width_shard:].astype(jnp.bfloat16)
    return (input_grad, down_grad, up_grad)


def solution(mesh):
    in_specs = (
        P("dp", "tensor"),
        P(("dp", "tensor"), None),
        P("tensor", None),
        P("dp", None, "tensor"),
        P("dp", None, "tensor"),
        P(),
        P(),
        P("dp"),
    )
    out_specs = (P("dp", "tensor"), P("dp", None, "tensor"), P("dp", None, "tensor"))
    return jax.shard_map(
        on_device, mesh=mesh, in_specs=in_specs, out_specs=out_specs, check_vma=False
    )
```

profile of v0, /device:TPU:25, one launch (start us, length us, event | category | flops | bytes accessed | tf_op | source)
XLA Modules:
  0.0 403.5 jit_solution(13323799420373628107)
XLA Ops:
  7.2 1.6 pad_maximum_fusion.2
  8.9 0.7 all-gather.3.cloned.1.call-update
  10.3 0.9 select_reduce_fusion
  11.4 45.4 %all-gather.5.cloned.1.call-done = bf16[128,16,288]{2,1,0:T(8,128)(2,1)} async-done(((bf16[8,16,288]{2,1,0:T(8,128)(2,1)}), bf16[128,16,288]{2,1,0:T(8,128)(2,1)}) %all-gather.5.cloned.1.call-update) | async-done | bytes 1179664 | tf_op jit(solution)/shard_map/all_gather | solution.py:37
  56.9 2.0 copy.26
  58.9 1.2 convolution_convert_fusion
  60.2 1.5 reshape.28
  61.7 1.4 convolution_bitcast_fusion
  63.1 100.0 %all-gather.3.cloned.1.call-done = bf16[4096,1024]{1,0:T(8,128)(2,1)} async-done(((bf16[128,1024]{1,0:T(8,128)(2,1)}), bf16[4096,1024]{1,0:T(8,128)(2,1)}) %all-gather.3.cloned.1.call-update) | async-done | bytes 8388624 | tf_op jit(solution)/shard_map/all_gather | solution.py:30
  163.0 4.5 %broadcast_select_fusion = bf16[4096,1024]{1,0:T(8,128)(2,1)S(1)} fusion(bf16[4096,1024]{1,0:T(8,128)(2,1)} %all-gather.3.cloned.1.call-done, pred[4096]{0:T(1024)(128)(4,1)S(1)} %broadcast_bitcast_fusion), kind=kLoop, calls=%fused_computation | loop fusion | flops 4194304 | bytes 16781312 | tf_op jit(solution)/shard_map/jit(_where)/select_n | solution.py:43
  167.5 3.2 copy-done.1
  170.7 0.4 constant_dynamic-slice_fusion
  171.1 0.6 convolution_bitcast_fusion.1
  171.7 0.9 pad_maximum_fusion.1
  172.7 151.7 %all-reduce.2.cloned.1.call-done = f32[2,32,16,128]{3,2,1,0:T(8,128)} async-done(((f32[2,32,16,128]{3,2,1,0:T(8,128)}), f32[2,32,16,128]{3,2,1,0:T(8,128)}) %all-reduce.2.cloned.1.call-update) | async-done | bytes 524304 | tf_op jit(solution)/shard_map/psum | solution.py:50
  324.4 1.1 reduce-precision_convert_fusion
  326.2 0.4 convolution_multiply_fusion.1
  326.6 3.2 convolution_reduce-precision_fusion
  329.9 0.8 convolution_multiply_fusion
  330.9 7.3 %fusion = bf16[4096,256]{1,0:T(8,128)(2,1)} fusion(f32[4096,256]{1,0:T(8,128)S(1)} %bitcast.34, bf16[4096,1024]{1,0:T(8,128)(2,1)} %copy-done.1, bf16[256,1024]{1,0:T(8,128)(2,1)S(1)} %copy-done.5), kind=kOutput, calls=%fused_computation.3 | convolution fusion | flops 2149580800 | bytes 15204352 | tf_op jit(solution)/shard_map/dot_general | solution.py:54
  338.2 56.6 %reduce-scatter.2.cloned.1.call-done = f32[8,16,288]{2,0,1:T(8,128)} async-done(((f32[128,16,288]{2,0,1:T(8,128)}), f32[8,16,288]{2,0,1:T(8,128)}) %reduce-scatter.2.cloned.1.call-update) | async-done | bytes 147472 | tf_op jit(solution)/shard_map/reduce_scatter | solution.py:69
  394.8 0.9 convert.9
  395.7 0.6 copy.31
  396.4 0.6 copy.32
  (25 shorter events, 1.4 us)
Async XLA Ops:
  7.2 54.5 %copy-start = (bf16[4096,256]{1,0:T(8,128)(2,1)S(1)}, bf16[4096,256]{1,0:T(8,128)(2,1)}, u32[]{:S(2)}) copy-start(bf16[4096,256]{1,0:T(8,128)(2,1)} %param.8) | copy-start | bytes 6291460
  7.2 49.7 %all-gather.5.cloned.1.call-start = ((), (), s32[]{:S(2)}) async-start(), calls=%async_computation.2 | async-start | bytes 1671168 | tf_op jit(solution)/shard_map/all_gather | solution.py:37
  8.9 154.1 %all-gather.3.cloned.1.call-start = ((), (), s32[]{:S(2)}) async-start(), calls=%async_computation.1 | async-start | bytes 8650752 | tf_op jit(solution)/shard_map/all_gather | solution.py:30
  9.6 314.8 %all-reduce.2.cloned.1.call-start = ((), (), s32[]{:S(2)}) async-start(), calls=%async_computation.3 | async-start | bytes 1048576 | tf_op jit(solution)/shard_map/psum | solution.py:50
  163.0 8.7 %copy-start.4 = (f32[1,32,16,128]{3,2,1,0:T(8,128)S(1)}, f32[1,32,16,128]{3,2,1,0:T(8,128)}, u32[]{:S(2)}) copy-start(f32[1,32,16,128]{3,2,1,0:T(8,128)} %convolution_bitcast_fusion) | copy-start | bytes 786436
  167.5 3.2 copy-start.1
  172.6 222.1 %reduce-scatter.2.cloned.1.call-start = ((), (), s32[]{:S(2)}) async-start(), calls=%async_computation.4 | async-start | bytes 3342336 | tf_op jit(solution)/shard_map/reduce_scatter | solution.py:69
  325.5 0.7 copy-start.2
  326.6 3.3 copy-start.3
  329.9 1.0 copy-start.5
Sparse Core Ops, SparseCore 0:
  10.7 46.1 all-gather.4
  60.0 102.9 all-gather.2
  172.7 151.6 all-reduce.1
  330.0 64.6 reduce-scatter.1
where the time goes:
time: 404 us
  waiting for transfers between devices  354 us (88%)
  matrix products  15.3 us (4%)
  between operations  14.5 us (4%)
  other arithmetic  9.97 us (2%)
  local copies, waits for them, and re-layouts  9.15 us (2%)
    psum x1, waiting for transfers between devices, on_device(): both = lax.psum(jnp.stack([up_part, down_part]), 'tensor')  152 us
    all_gather x1, waiting for transfers between devices, on_device(): whole_raw = lax.all_gather(output_grad, 'tensor', axis=0, tiled=True)  100 us
    reduce_scatter x1, waiting for transfers between devices, on_device(): total = lax.psum_scatter(part, 'dp', scatter_dimension=0, tiled=True)  56.6 us
    all_gather x1, waiting for transfers between devices, on_device(): stores = lax.all_gather(local_store, 'dp', axis=0, tiled=True)  45.4 us
  transfers between devices with their start and end apart: 4, of which 4 were waited for; matrix products, arithmetic and copies ran while one was open for 4% of the time, Pallas kernels for 0%

commit v1 on v0

--- a/solution.py
+++ b/solution.py
@@ -34,7 +34,9 @@
     seg_slot = lax.dynamic_slice_in_dim(every_slot, group_index * seg_group, seg_group)
     seg_live = jnp.arange(seg_group, dtype=jnp.int32) < live_segments[0]
     local_store = jnp.concatenate([adapter_down, adapter_up], axis=2)
-    stores = lax.all_gather(local_store, "dp", axis=0, tiled=True)
+    stores = jnp.concatenate(
+        lax.all_to_all(jnp.stack([local_store] * lax.axis_size("dp")), "dp", 0, 0), axis=0
+    )
     choose = (seg_slot[:, None] == slot_ids[None, :]).astype(jnp.bfloat16)
     seg_store = jnp.dot(choose, stores.reshape(adapters, -1), preferred_element_type=jnp.float32)
     seg_store = seg_store.astype(jnp.bfloat16).reshape(seg_group, rank_dim, width_shard + key_shard)

time: 404 us -> 361 us (0.89)
  waiting for transfers between devices: 354 us -> 301 us
  starting transfers between devices: 0.16 us -> 10.2 us
    all_gather x1 -> x0, waiting for transfers between devices: 45.4 us -> none  [on_device(): stores = lax.all_gather(local_store, 'dp', axis=0, tiled=True)]
    all_gather x1, waiting for transfers between devices: 100 us -> 55.1 us  [on_device(): whole_raw = lax.all_gather(output_grad, 'tensor', axis=0, tiled=True)]
    all_to_all x0 -> x1, waiting for transfers between devices: none -> 36.5 us  [on_device(): lax.all_to_all(jnp.stack([local_store] * lax.axis_size('dp')), 'dp', 0, 0)]
    all_to_all x0 -> x1, starting transfers between devices: none -> 10.1 us  [on_device(): lax.all_to_all(jnp.stack([local_store] * lax.axis_size('dp')), 'dp', 0, 0)]
    another operation x0 -> x2, local copies, waits for them, and re-layouts: none -> 4.31 us  [the longest x1 2.96 us: on_device(): stores.reshape(adapters, -1)]
  transfers between devices with their start and end apart: 4 -> 4, of which waited for: 4 -> 4; matrix products, arithmetic and copies ran while one was open for 4% -> 5% of each run, Pallas kernels for 0% -> 0%
where the time goes in v1:
time: 361 us; the launch traced here: 360 us
  waiting for transfers between devices  301 us (83%)
  matrix products  15.1 us (4%)
  between operations  14.6 us (4%)
  local copies, waits for them, and re-layouts  11.5 us (3%)
  starting transfers between devices  10.2 us (3%)
  other arithmetic  8.46 us (2%)
    psum x1, waiting for transfers between devices, on_device(): both = lax.psum(jnp.stack([up_part, down_part]), 'tensor')  152 us
    reduce_scatter x1, waiting for transfers between devices, on_device(): total = lax.psum_scatter(part, 'dp', scatter_dimension=0, tiled=True)  56.5 us
    all_gather x1, waiting for transfers between devices, on_device(): whole_raw = lax.all_gather(output_grad, 'tensor', axis=0, tiled=True)  55.1 us
    all_to_all x1, waiting for transfers between devices, on_device(): lax.all_to_all(jnp.stack([local_store] * lax.axis_size('dp')), 'dp', 0, 0)  36.5 us
    all_to_all x1, starting transfers between devices, on_device(): lax.all_to_all(jnp.stack([local_store] * lax.axis_size('dp')), 'dp', 0, 0)  10.1 us
    dot_general x1, matrix products, on_device(): lax.dot_general(whole, key_weight, (((1,), (1,)), ((), ())), preferred_el...  7.29 us
  transfers between devices with their start and end apart: 4, of which 4 were waited for; matrix products, arithmetic and copies ran while one was open for 5% of the time, Pallas kernels for 0%

profile of v1, /device:TPU:25, one launch (start us, length us, event | category | flops | bytes accessed | tf_op | source)
XLA Modules:
  0.0 360.4 jit_solution(342454628477226473)
XLA Ops:
  7.2 0.7 all-gather.2.cloned.1.call-update
  7.9 0.9 pad_maximum_fusion.2
  8.8 1.3 stack.8
  10.2 10.1 %all-to-all-start = ((bf16[16,8,16,288]{3,2,1,0:T(8,128)(2,1)}), bf16[16,8,16,288]{3,2,1,0:T(8,128)(2,1)}, u32[]{:S(2)}, u32[]{:S(2)}) async-start(bf16[16,8,16,288]{3,2,1,0:T(8,128)(2,1)} %stack.8), calls=%async_computation | async-start | bytes 3145728 | tf_op jit(solution)/shard_map/all_to_all | solution.py:38
  21.4 36.5 %all-to-all-done = bf16[16,8,16,288]{3,2,1,0:T(8,128)(2,1)} async-done(((bf16[16,8,16,288]{3,2,1,0:T(8,128)(2,1)}), bf16[16,8,16,288]{3,2,1,0:T(8,128)(2,1)}, u32[]{:S(2)}, u32[]{:S(2)}) %all-to-all-start) | async-done | bytes 1179680 | tf_op jit(solution)/shard_map/all_to_all | solution.py:38
  57.9 3.0 reshape_reshape.3
  60.9 1.1 convolution_convert_fusion
  61.9 1.5 reshape.26
  63.5 1.4 convolution_bitcast_fusion
  64.8 55.1 %all-gather.2.cloned.1.call-done = bf16[4096,1024]{1,0:T(8,128)(2,1)} async-done(((bf16[128,1024]{1,0:T(8,128)(2,1)}), bf16[4096,1024]{1,0:T(8,128)(2,1)}) %all-gather.2.cloned.1.call-update) | async-done | bytes 8388624 | tf_op jit(solution)/shard_map/all_gather | solution.py:30
  119.9 4.4 %broadcast_select_fusion = bf16[4096,1024]{1,0:T(8,128)(2,1)S(1)} fusion(bf16[4096,1024]{1,0:T(8,128)(2,1)} %all-gather.2.cloned.1.call-done, pred[4096]{0:T(1024)(128)(4,1)S(1)} %broadcast_bitcast_fusion), kind=kLoop, calls=%fused_computation | loop fusion | flops 4194304 | bytes 16781312 | tf_op jit(solution)/shard_map/jit(_where)/select_n | solution.py:45
  124.4 3.2 copy-done.1
  127.6 0.4 constant_dynamic-slice_fusion
  128.0 0.6 convolution_bitcast_fusion.1
  128.6 0.9 pad_maximum_fusion.1
  129.6 151.7 %all-reduce.2.cloned.1.call-done = f32[2,32,16,128]{3,2,1,0:T(8,128)} async-done(((f32[2,32,16,128]{3,2,1,0:T(8,128)}), f32[2,32,16,128]{3,2,1,0:T(8,128)}) %all-reduce.2.cloned.1.call-update) | async-done | bytes 524304 | tf_op jit(solution)/shard_map/psum | solution.py:52
  281.3 1.1 reduce-precision_convert_fusion
  283.5 3.2 convolution_reduce-precision_fusion
  286.8 0.7 convolution_multiply_fusion
  287.8 7.3 %fusion = bf16[4096,256]{1,0:T(8,128)(2,1)} fusion(f32[4096,256]{1,0:T(8,128)S(1)} %bitcast.34, bf16[4096,1024]{1,0:T(8,128)(2,1)} %copy-done.1, bf16[256,1024]{1,0:T(8,128)(2,1)S(1)} %copy-done.7), kind=kOutput, calls=%fused_computation.3 | convolution fusion | flops 2149580800 | bytes 15204352 | tf_op jit(solution)/shard_map/dot_general | solution.py:56
  295.1 56.5 %reduce-scatter.2.cloned.1.call-done = f32[8,16,288]{2,0,1:T(8,128)} async-done(((f32[128,16,288]{2,0,1:T(8,128)}), f32[8,16,288]{2,0,1:T(8,128)}) %reduce-scatter.2.cloned.1.call-update) | async-done | bytes 147472 | tf_op jit(solution)/shard_map/reduce_scatter | solution.py:71
  351.7 0.9 convert.9
  352.6 0.6 copy.21
  353.3 0.6 copy.22
  (29 shorter events, 2.0 us)
Async XLA Ops:
  7.2 56.3 %copy-start = (bf16[4096,256]{1,0:T(8,128)(2,1)S(1)}, bf16[4096,256]{1,0:T(8,128)(2,1)}, u32[]{:S(2)}) copy-start(bf16[4096,256]{1,0:T(8,128)(2,1)} %param.8) | copy-start | bytes 6291460
  7.2 13.8 %copy-start.6 = (s32[128]{0:T(128)S(1)}, s32[128]{0:T(128)}, u32[]{:S(2)}) copy-start(s32[128]{0:T(128)} %param.14) | copy-start | bytes 1540
  7.2 13.8 %copy-start.5 = (s32[512]{0:T(512)S(1)}, s32[512]{0:T(512)}, u32[]{:S(2)}) copy-start(s32[512]{0:T(512)} %param.13) | copy-start | bytes 6148
  7.2 112.7 %all-gather.2.cloned.1.call-start = ((), (), s32[]{:S(2)}) async-start(), calls=%async_computation.2 | async-start | bytes 8650752 | tf_op jit(solution)/shard_map/all_gather | solution.py:30
  10.2 47.7 %all-to-all-start = ((bf16[16,8,16,288]{3,2,1,0:T(8,128)(2,1)}), bf16[16,8,16,288]{3,2,1,0:T(8,128)(2,1)}, u32[]{:S(2)}, u32[]{:S(2)}) async-start(bf16[16,8,16,288]{3,2,1,0:T(8,128)(2,1)} %stack.8), calls=%async_computation | async-start | bytes 3145728 | tf_op jit(solution)/shard_map/all_to_all | solution.py:38
  20.3 261.0 %all-reduce.2.cloned.1.call-start = ((), (), s32[]{:S(2)}) async-start(), calls=%async_computation.3 | async-start | bytes 1048576 | tf_op jit(solution)/shard_map/psum | solution.py:52
  124.4 3.2 copy-start.1
  127.6 1.0 copy-start.4
  129.5 222.2 %reduce-scatter.2.cloned.1.call-start = ((), (), s32[]{:S(2)}) async-start(), calls=%async_computation.4 | async-start | bytes 3342336 | tf_op jit(solution)/shard_map/reduce_scatter | solution.py:71
  282.4 0.7 copy-start.2
  283.5 3.3 copy-start.3
  286.8 1.0 copy-start.7
Sparse Core Ops, SparseCore 0:
  11.2 108.6 all-gather.1
  129.6 151.6 all-reduce.1
  286.9 64.6 reduce-scatter.1
